TPU v7x, 512 devices: a whole 4x8x8 slice. The times are simulated.
512 devices in a mesh: row: 64 (over z, y), col: 8 (over x, core).
Axes of the slice: x: 4, y: 8, z: 8, core: 2. Of those that a mesh axis runs over, the one named last changes fastest.
Arguments:
- tiles: float32 [64, 8, 64, 128, 128], P('row', 'col'), may hold values from -0.0625 to 0.0625
- tile_rows: int32 [64, 8, 64], P('row', 'col'), may hold values from 0 to 15, as said below
- tile_cols: int32 [64, 8, 64], P('row', 'col'), may hold values from 0 to 63, as said below
- exponents: int32 [65536], P('col'), may hold values from 0 to 3
- u_basis: float32 [64, 131072], P(None, 'row'), may hold values from -6 to 6
- v_basis: float32 [64, 65536], P(None, ('col', 'row')), may hold values from -6 to 6
- prior: float32 [64, 64], replicated, may hold values from -0.75 to 0.75
Outputs:
- u_next: float32 [64, 131072], P(None, ('row', 'col'))
- v_next: float32 [64, 65536], P(None, ('col', 'row'))
- v_factor: float32 [64, 64], replicated
- u_factor: float32 [64, 64], replicated
Inputs may be any that keep to these rules, and one draw needn't show every extreme that they name: `tile_rows`: within each grid cell every tile row of 0 to 15 appears exactly 64 / 16 times. `tile_cols`: within each grid cell every tile column of 0 to 63 appears exactly 64 / 64 times.
All inputs are finite; a program needn't handle non-finite values.
Results may differ from a plain program's by a relative error of at most 0.00018.
Values sent between devices are 32-bit elements; how exact they have to be, the bound alone decides.
No kernel may reach another device: no remote copies, remote signals or barrier semaphores. Data moves between devices by JAX's collectives and lax.ppermute only.
A program may use at most 64 MiB of HBM per device.

v0:
```python
import math
import jax
import jax.numpy as jnp
from jax import lax
from jax.sharding import PartitionSpec as P

HIGH = lax.Precision.HIGHEST


def lower_solve(factor, rhs):
    return lax.linalg.triangular_solve(factor, rhs, left_side=True, lower=True)


def per_device(tiles, tile_rows, tile_cols, exponents, u_basis, v_basis, prior):
    local_tiles = tiles[0, 0]
    rows_here = tile_rows[0, 0]
    cols_here = tile_cols[0, 0]
    count, tl, _ = local_tiles.shape
    width, block_rows = u_basis.shape
    block_cols = exponents.shape[0]
    rows_tiles = block_rows // tl
    cols_tiles = block_cols // tl
    total_rows = block_rows * lax.axis_size("row")
    total_cols = block_cols * lax.axis_size("col")
    v_piece = v_basis.shape[1]
    u_piece = block_rows // lax.axis_size("col")
    col_scale = jnp.exp2(-exponents.astype(jnp.float32))
    lowtri = jnp.tril(prior)
    col_hits = (cols_here[:, None] == jnp.arange(cols_tiles, dtype=jnp.int32)[None, :]).astype(
        jnp.float32
    )
    row_hits = (rows_here[:, None] == jnp.arange(rows_tiles, dtype=jnp.int32)[None, :]).astype(
        jnp.float32
    )
    picked = jnp.take(u_basis.reshape(width, rows_tiles, tl), rows_here, axis=1)
    prod = jnp.einsum("sta,tab->stb", picked, local_tiles, precision=HIGH)
    partial_value = (
        jnp.einsum("stb,tc->scb", prod, col_hits, precision=HIGH).reshape(width, block_cols)
        * col_scale
    )
    offset = lax.axis_index("row") * v_piece
    own_term = jnp.dot(lowtri, v_basis, precision=HIGH)
    slot = lax.dynamic_slice_in_dim(partial_value, offset, v_piece, 1) - own_term
    partial_value = lax.dynamic_update_slice_in_dim(partial_value, slot, offset, 1)
    pt_piece = lax.psum_scatter(partial_value, "row", scatter_dimension=1, tiled=True)
    gram = lax.psum(jnp.dot(pt_piece, pt_piece.T, precision=HIGH), ("row", "col"))
    v_factor = jnp.linalg.cholesky(gram / total_cols)
    v_next = lower_solve(v_factor, pt_piece)
    source = lax.all_gather(v_next, "row", axis=1, tiled=True)
    factor = math.sqrt(total_rows / total_cols)
    scaled = (source * col_scale).reshape(width, cols_tiles, tl)
    chosen = jnp.take(scaled, cols_here, axis=1)
    products = jnp.einsum("stb,tab->sta", chosen, local_tiles, precision=HIGH)
    terms = factor * jnp.einsum("sta,tr->sra", products, row_hits, precision=HIGH).reshape(
        width, block_rows
    )
    summed = lax.psum_scatter(terms, "col", scatter_dimension=1, tiled=True)
    u_own = lax.dynamic_slice_in_dim(u_basis, lax.axis_index("col") * u_piece, u_piece, 1)
    qt_piece = summed - jnp.dot(v_factor.T, u_own, precision=HIGH)
    ugram = lax.psum(jnp.dot(qt_piece, qt_piece.T, precision=HIGH), ("row", "col"))
    u_factor = jnp.linalg.cholesky(ugram / total_rows)
    u_next = lower_solve(u_factor, qt_piece)
    return (u_next, v_next, v_factor, u_factor)


def solution(mesh):
    placed = (
        P("row", "col", None, None, None),
        P("row", "col", None),
        P("row", "col", None),
        P("col"),
        P(None, "row"),
        P(None, ("col", "row")),
        P(),
    )
    return jax.shard_map(
        per_device,
        mesh=mesh,
        in_specs=placed,
        out_specs=(P(None, ("row", "col")), P(None, ("col", "row")), P(), P()),
        check_vma=False,
    )
```

profile of v0, /device:TPU:1, one launch (start us, length us, event | category | flops | bytes accessed | tf_op | source)
XLA Modules:
  0.0 630.2 jit_solution(3144894267777404665)
XLA Ops:
  8.7 0.8 multiply_exponential_fusion
  10.2 5.7 fusion.12
  15.9 2.5 fusion.8
  18.4 1.2 bitcast_multiply_fusion
  19.8 1.3 copy-done.1
  21.2 246.1 %reduce-scatter.3.cloned.1.call-done = f32[64,128]{1,0:T(8,128)} async-done(((f32[64,8192]{1,0:T(8,128)}), f32[64,128]{1,0:T(8,128)}) %reduce-scatter.3.cloned.1.call-update) | async-done | bytes 32784 | tf_op jit(solution)/shard_map/reduce_scatter | solution.py:45
  267.3 1.0 fusion.53
  268.3 99.8 %psum.14 = f32[64,64]{0,1:T(8,128)S(1)} all-reduce(f32[64,64]{0,1:T(8,128)S(1)} %fusion.53), channel_id=1, replica_groups=mesh['row'=64,'col'=8] {'row','col'}, use_global_device_ids=true, to_apply=%region_1.2 | all-reduce | flops 4096 | bytes 32768 | tf_op jit(solution)/shard_map/psum | solution.py:46
  368.2 5.8 cholesky.44
  375.4 4.9 custom-call.8
  380.3 1.6 fusion.34
  382.2 76.0 %all-gather.2.cloned.1.call-done = f32[64,8192]{1,0:T(8,128)} async-done(((f32[64,128]{1,0:T(8,128)}), f32[64,8192]{1,0:T(8,128)}) %all-gather.2.cloned.1.call-update) | async-done | bytes 2097168 | tf_op jit(solution)/shard_map/all_gather | solution.py:49
  458.2 1.9 copy_bitcast_fusion
  460.1 2.0 gather_fusion.1
  462.1 10.1 %fusion.17 = f32[64,64,128]{2,0,1:T(8,128)S(1)} fusion(f32[1,1,64,128,128]{4,3,2,1,0:T(8,128)} %param.8, f32[64,64,128]{2,1,0:T(8,128)} %gather_fusion.1, pred[64]{0:T(512)(128)(4,1)S(1)} %get-tuple-element.10), kind=kOutput, calls=%fused_computation.18 | convolution fusion | flops 805830656 | bytes 8388672 | tf_op jit(solution)/shard_map/stb,tab->sta/dot_general | solution.py:53
  472.2 2.0 fusion.22
  474.2 1.0 copy.44
  475.2 34.1 %reduce-scatter.5.cloned.1.call-done = f32[64,256]{1,0:T(8,128)} async-done(((f32[64,2048]{1,0:T(8,128)}), f32[64,256]{1,0:T(8,128)}) %reduce-scatter.5.cloned.1.call-update) | async-done | bytes 65552 | tf_op jit(solution)/shard_map/reduce_scatter | solution.py:57
  509.3 1.1 convolution_subtract_fusion
  510.6 99.4 %psum.15 = f32[64,64]{0,1:T(8,128)S(1)} all-reduce(f32[64,64]{0,1:T(8,128)S(1)} %fusion.54), channel_id=1, replica_groups=mesh['row'=64,'col'=8] {'row','col'}, use_global_device_ids=true, to_apply=%region_5.7 | all-reduce | flops 4096 | bytes 32768 | tf_op jit(solution)/shard_map/psum | solution.py:60
  610.1 5.8 cholesky.55
  616.6 1.3 select_bitcast_fusion
  617.9 4.9 custom-call.9
  622.8 0.9 fusion.31
  (39 shorter events, 5.1 us)
Async XLA Ops:
  7.2 1.5 copy-start
  7.2 260.1 %reduce-scatter.3.cloned.1.call-start = ((), (), s32[]{:S(2)}) async-start(), calls=%async_computation.2 | async-start | bytes 2129920 | tf_op jit(solution)/shard_map/reduce_scatter | solution.py:45
  10.2 5.7 copy-start.5
  18.4 1.2 copy-start.3
  18.4 1.2 copy-start.4
  19.8 1.4 copy-start.1
  21.2 437.0 %all-gather.2.cloned.1.call-start = ((), (), s32[]{:S(2)}) async-start(), calls=%async_computation.3 | async-start | bytes 2129920 | tf_op jit(solution)/shard_map/all_gather | solution.py:49
  375.4 133.9 %copy-start.2 = (f32[64,64]{1,0:T(8,128)}, f32[64,64]{1,0:T(8,128)S(1)}, u32[]{:S(2)}) copy-start(f32[64,64]{1,0:T(8,128)S(1)} %get-tuple-element.8) | copy-start | bytes 49156
  382.0 127.3 %reduce-scatter.5.cloned.1.call-start = ((), (), s32[]{:S(2)}) async-start(), calls=%async_computation.4 | async-start | bytes 589824 | tf_op jit(solution)/shard_map/reduce_scatter | solution.py:57
  462.1 10.1 %copy-start.6 = (s32[1,1,64]{2,1,0:T(1,128)S(1)}, s32[1,1,64]{2,1,0:T(1,128)}, u32[]{:S(2)}) copy-start(s32[1,1,64]{2,1,0:T(1,128)} %param.9) | copy-start | bytes 772
Sparse Core Ops, SparseCore 0:
  21.3 245.9 reduce-scatter.2
  382.1 76.0 all-gather.1
  475.3 33.9 reduce-scatter.4
where the time goes:
time: 631 us; the launch traced here: 630 us
  waiting for transfers between devices  356 us (56%)
  blocking collectives  199 us (32%)
  other arithmetic  30 us (5%)
  matrix products  25.2 us (4%)
  between operations  14 us (2%)
    reduce_scatter x1, waiting for transfers between devices, per_device(): lax.psum_scatter(partial_value, 'row', scatter_dimension=1, tiled=True)  246 us
    psum x1, blocking collectives, per_device(): lax.psum(jnp.dot(pt_piece, pt_piece.T, precision=HIGH), ('row', 'col'))  99.8 us
    psum x1, blocking collectives, per_device(): lax.psum(jnp.dot(qt_piece, qt_piece.T, precision=HIGH), ('row', 'col'))  99.4 us
    all_gather x1, waiting for transfers between devices, per_device(): source = lax.all_gather(v_next, 'row', axis=1, tiled=True)  76 us
    reduce_scatter x1, waiting for transfers between devices, per_device(): summed = lax.psum_scatter(terms, 'col', scatter_dimension=1, tiled=True)  34.1 us
  transfers between devices with their start and end apart: 3, of which 3 were waited for; matrix products, arithmetic and copies ran while one was open for 0% of the time, Pallas kernels for 0%

commit v1 on v0

--- a/solution.py
+++ b/solution.py
@@ -57,7 +57,9 @@
     summed = lax.psum_scatter(terms, "col", scatter_dimension=1, tiled=True)
     u_own = lax.dynamic_slice_in_dim(u_basis, lax.axis_index("col") * u_piece, u_piece, 1)
     qt_piece = summed - jnp.dot(v_factor.T, u_own, precision=HIGH)
-    ugram = lax.psum(jnp.dot(qt_piece, qt_piece.T, precision=HIGH), ("row", "col"))
+    ugram = jnp.sum(
+        lax.all_gather(jnp.dot(qt_piece, qt_piece.T, precision=HIGH), ("row", "col")), axis=0
+    )
     u_factor = jnp.linalg.cholesky(ugram / total_rows)
     u_next = lower_solve(u_factor, qt_piece)
     return (u_next, v_next, v_factor, u_factor)

time: 631 us -> 678 us (1.074)
  waiting for transfers between devices: 356 us -> 495 us
  blocking collectives: 199 us -> 99.9 us
  other arithmetic: 30 us -> 37 us
    all_gather x0 -> x1, waiting for transfers between devices: none -> 139 us  [per_device(): lax.all_gather(jnp.dot(qt_piece, qt_piece.T, precision=HIGH), ('row', 'co...]
    psum x1 -> x0, blocking collectives: 99.4 us -> none  [per_device(): lax.psum(jnp.dot(qt_piece, qt_piece.T, precision=HIGH), ('row', 'col'))]
    reduce_sum x0 -> x1, other arithmetic: none -> 6.94 us  [per_device(): jnp.sum(lax.all_gather(jnp.dot(qt_piece, qt_piece.T, precision=HIGH), ('r...]
  transfers between devices with their start and end apart: 3 -> 4, of which waited for: 3 -> 4; matrix products, arithmetic and copies ran while one was open for 0% -> 0% of each run, Pallas kernels for 0% -> 0%
where the time goes in v1:
time: 678 us
  waiting for transfers between devices  495 us (73%)
  blocking collectives  99.9 us (15%)
  other arithmetic  37 us (5%)
  matrix products  25.8 us (4%)
  between operations  14 us (2%)
    reduce_scatter x1, waiting for transfers between devices, per_device(): lax.psum_scatter(partial_value, 'row', scatter_dimension=1, tiled=True)  246 us
    all_gather x1, waiting for transfers between devices, per_device(): lax.all_gather(jnp.dot(qt_piece, qt_piece.T, precision=HIGH), ('row', 'co...  139 us
    psum x1, blocking collectives, per_device(): lax.psum(jnp.dot(pt_piece, pt_piece.T, precision=HIGH), ('row', 'col'))  99.9 us
    all_gather x1, waiting for transfers between devices, per_device(): source = lax.all_gather(v_next, 'row', axis=1, tiled=True)  75.9 us
    reduce_scatter x1, waiting for transfers between devices, per_device(): summed = lax.psum_scatter(terms, 'col', scatter_dimension=1, tiled=True)  34 us
  transfers between devices with their start and end apart: 4, of which 4 were waited for; matrix products, arithmetic and copies ran while one was open for 0% of the time, Pallas kernels for 0%

profile of v1, /device:TPU:1, one launch (start us, length us, event | category | flops | bytes accessed | tf_op | source)
XLA Modules:
  0.0 677.9 jit_solution(15229569567738899813)
XLA Ops:
  10.2 5.7 fusion.12
  15.9 2.5 fusion.8
  18.4 1.2 bitcast_multiply_fusion
  19.8 1.3 copy-done.1
  21.2 246.1 %reduce-scatter.3.cloned.1.call-done = f32[64,128]{1,0:T(8,128)} async-done(((f32[64,8192]{1,0:T(8,128)}), f32[64,128]{1,0:T(8,128)}) %reduce-scatter.3.cloned.1.call-update) | async-done | bytes 32784 | tf_op jit(solution)/shard_map/reduce_scatter | solution.py:45
  267.3 1.0 fusion.53
  268.3 99.9 %psum.7 = f32[64,64]{0,1:T(8,128)S(1)} all-reduce(f32[64,64]{0,1:T(8,128)S(1)} %fusion.53), channel_id=1, replica_groups=mesh['row'=64,'col'=8] {'row','col'}, use_global_device_ids=true, to_apply=%region_1.2 | all-reduce | flops 4096 | bytes 32768 | tf_op jit(solution)/shard_map/psum | solution.py:46
  368.3 5.8 cholesky.44
  375.5 4.9 custom-call.8
  380.4 1.6 fusion.34
  382.3 75.9 %all-gather.4.cloned.1.call-done = f32[64,8192]{1,0:T(8,128)} async-done(((f32[64,128]{1,0:T(8,128)}), f32[64,8192]{1,0:T(8,128)}) %all-gather.4.cloned.1.call-update) | async-done | bytes 2097168 | tf_op jit(solution)/shard_map/all_gather | solution.py:49
  458.2 1.9 copy_bitcast_fusion
  460.1 2.0 gather_fusion.1
  462.2 10.1 %fusion.17 = f32[64,64,128]{2,0,1:T(8,128)S(1)} fusion(f32[1,1,64,128,128]{4,3,2,1,0:T(8,128)} %param.8, f32[64,64,128]{2,1,0:T(8,128)} %gather_fusion.1, pred[64]{0:T(512)(128)(4,1)S(1)} %get-tuple-element.10), kind=kOutput, calls=%fused_computation.18 | convolution fusion | flops 805830656 | bytes 8388672 | tf_op jit(solution)/shard_map/stb,tab->sta/dot_general | solution.py:53
  472.3 2.0 fusion.22
  474.2 1.0 copy.48
  475.3 34.0 %reduce-scatter.5.cloned.1.call-done = f32[64,256]{1,0:T(8,128)} async-done(((f32[64,2048]{1,0:T(8,128)}), f32[64,256]{1,0:T(8,128)}) %reduce-scatter.5.cloned.1.call-update) | async-done | bytes 65552 | tf_op jit(solution)/shard_map/reduce_scatter | solution.py:57
  509.3 1.1 convolution_subtract_fusion
  511.3 139.3 %all-gather.6.cloned.1.call-done = f32[32768,64]{1,0:T(8,128)} async-done(((f32[64,64]{1,0:T(8,128)}), f32[32768,64]{1,0:T(8,128)}) %all-gather.6.cloned.1.call-update) | async-done | bytes 8388624 | tf_op jit(solution)/shard_map/all_gather | solution.py:61
  650.6 6.9 %reduce_sum.9 = f32[64,64]{1,0:T(8,128)S(1)} reduce(f32[512,64,64]{2,1,0:T(8,128)} %bitcast.87, f32[]{:T(128)} %constant.89.clone.1), dimensions={0}, to_apply=%region_5.7 | reduce | flops 2093056 | bytes 8404996 | tf_op jit(solution)/shard_map/reduce_sum | solution.py:60
  657.7 5.8 cholesky.55
  664.3 1.3 select_bitcast_fusion
  665.5 4.9 custom-call.9
  670.4 0.9 fusion.31
  (43 shorter events, 6.6 us)
Async XLA Ops:
  7.2 2.2 copy-start
  7.2 260.1 %reduce-scatter.3.cloned.1.call-start = ((), (), s32[]{:S(2)}) async-start(), calls=%async_computation.2 | async-start | bytes 2129920 | tf_op jit(solution)/shard_map/reduce_scatter | solution.py:45
  10.2 5.7 copy-start.5
  18.4 1.2 copy-start.3
  18.4 1.2 copy-start.4
  19.8 1.4 copy-start.1
  21.2 437.1 %all-gather.4.cloned.1.call-start = ((), (), s32[]{:S(2)}) async-start(), calls=%async_computation.3 | async-start | bytes 2129920 | tf_op jit(solution)/shard_map/all_gather | solution.py:49
  375.5 133.8 %copy-start.2 = (f32[64,64]{1,0:T(8,128)}, f32[64,64]{1,0:T(8,128)S(1)}, u32[]{:S(2)}) copy-start(f32[64,64]{1,0:T(8,128)S(1)} %get-tuple-element.8) | copy-start | bytes 49156
  382.1 127.2 %reduce-scatter.5.cloned.1.call-start = ((), (), s32[]{:S(2)}) async-start(), calls=%async_computation.4 | async-start | bytes 589824 | tf_op jit(solution)/shard_map/reduce_scatter | solution.py:57
  462.2 10.1 %copy-start.6 = (s32[1,1,64]{2,1,0:T(1,128)S(1)}, s32[1,1,64]{2,1,0:T(1,128)}, u32[]{:S(2)}) copy-start(s32[1,1,64]{2,1,0:T(1,128)} %param.9) | copy-start | bytes 772
  475.2 175.4 %all-gather.6.cloned.1.call-start = ((), (), s32[]{:S(2)}) async-start(), calls=%async_computation.5 | async-start | bytes 16809984 | tf_op jit(solution)/shard_map/all_gather | solution.py:61
Sparse Core Ops, SparseCore 0:
  21.3 245.9 reduce-scatter.2
  382.2 75.9 all-gather.3
  475.3 33.9 reduce-scatter.4
  514.4 136.1 all-gather.5

commit v2 on v0

--- a/solution.py
+++ b/solution.py
@@ -43,7 +43,7 @@
     slot = lax.dynamic_slice_in_dim(partial_value, offset, v_piece, 1) - own_term
     partial_value = lax.dynamic_update_slice_in_dim(partial_value, slot, offset, 1)
     pt_piece = lax.psum_scatter(partial_value, "row", scatter_dimension=1, tiled=True)
-    gram = lax.psum(jnp.dot(pt_piece, pt_piece.T, precision=HIGH), ("row", "col"))
+    gram = lax.psum(lax.psum(jnp.dot(pt_piece, pt_piece.T, precision=HIGH), "row"), "col")
     v_factor = jnp.linalg.cholesky(gram / total_cols)
     v_next = lower_solve(v_factor, pt_piece)
     source = lax.all_gather(v_next, "row", axis=1, tiled=True)

time: 631 us -> 832 us (1.32)
  blocking collectives: 199 us -> 401 us
    psum x1 -> x2, blocking collectives: 99.8 us -> 302 us  [the longest x1 222 us: per_device(): lax.psum(jnp.dot(pt_piece, pt_piece.T, precision=HIGH), 'row')]
where the time goes in v2:
time: 832 us; the launch traced here: 831 us
  blocking collectives  401 us (48%)
  waiting for transfers between devices  355 us (43%)
  other arithmetic  30.1 us (4%)
  matrix products  25.2 us (3%)
  between operations  14 us (2%)
    reduce_scatter x1, waiting for transfers between devices, per_device(): lax.psum_scatter(partial_value, 'row', scatter_dimension=1, tiled=True)  246 us
    psum x1, blocking collectives, per_device(): lax.psum(jnp.dot(pt_piece, pt_piece.T, precision=HIGH), 'row')  222 us
    psum x1, blocking collectives, per_device(): lax.psum(jnp.dot(qt_piece, qt_piece.T, precision=HIGH), ('row', 'col'))  99.4 us
    psum x1, blocking collectives, per_device(): lax.psum(lax.psum(jnp.dot(pt_piece, pt_piece.T, precision=HIGH), 'row'),...  80 us
    all_gather x1, waiting for transfers between devices, per_device(): source = lax.all_gather(v_next, 'row', axis=1, tiled=True)  74.6 us
    reduce_scatter x1, waiting for transfers between devices, per_device(): summed = lax.psum_scatter(terms, 'col', scatter_dimension=1, tiled=True)  34.1 us
  transfers between devices with their start and end apart: 3, of which 3 were waited for; matrix products, arithmetic and copies ran while one was open for 0% of the time, Pallas kernels for 0%

profile of v2, /device:TPU:1, one launch (start us, length us, event | category | flops | bytes accessed | tf_op | source)
XLA Modules:
  0.0 831.0 jit_solution(2203086661720126701)
XLA Ops:
  10.2 5.7 fusion.12
  15.9 2.5 fusion.8
  18.4 1.2 bitcast_multiply_fusion
  19.8 1.3 copy-done.1
  21.2 246.1 %reduce-scatter.3.cloned.1.call-done = f32[64,128]{1,0:T(8,128)} async-done(((f32[64,8192]{1,0:T(8,128)}), f32[64,128]{1,0:T(8,128)}) %reduce-scatter.3.cloned.1.call-update) | async-done | bytes 32784 | tf_op jit(solution)/shard_map/reduce_scatter | solution.py:45
  267.3 1.0 fusion.53
  268.3 222.0 %psum.21 = f32[64,64]{0,1:T(8,128)S(1)} all-reduce(f32[64,64]{0,1:T(8,128)S(1)} %fusion.53), channel_id=1, replica_groups=mesh['row'=64,'col'=8] {'row'}, use_global_device_ids=true, to_apply=%region_1.2 | all-reduce | flops 4096 | bytes 32768 | tf_op jit(solution)/shard_map/psum | solution.py:46
  490.3 80.0 %psum.22 = f32[64,64]{0,1:T(8,128)S(1)} all-reduce(f32[64,64]{0,1:T(8,128)S(1)} %psum.21), channel_id=1, replica_groups=mesh['row'=64,'col'=8] {'col'}, use_global_device_ids=true, to_apply=%region_2.3 | all-reduce | flops 4096 | bytes 32768 | tf_op jit(solution)/shard_map/psum | solution.py:46
  570.4 5.8 cholesky.44
  577.6 4.9 custom-call.8
  582.5 1.6 fusion.34
  584.4 74.6 %all-gather.2.cloned.1.call-done = f32[64,8192]{1,0:T(8,128)} async-done(((f32[64,128]{1,0:T(8,128)}), f32[64,8192]{1,0:T(8,128)}) %all-gather.2.cloned.1.call-update) | async-done | bytes 2097168 | tf_op jit(solution)/shard_map/all_gather | solution.py:49
  659.0 1.9 copy_bitcast_fusion
  660.9 2.0 gather_fusion.1
  662.9 10.1 %fusion.17 = f32[64,64,128]{2,0,1:T(8,128)S(1)} fusion(f32[1,1,64,128,128]{4,3,2,1,0:T(8,128)} %param.8, f32[64,64,128]{2,1,0:T(8,128)} %gather_fusion.1, pred[64]{0:T(512)(128)(4,1)S(1)} %get-tuple-element.10), kind=kOutput, calls=%fused_computation.18 | convolution fusion | flops 805830656 | bytes 8388672 | tf_op jit(solution)/shard_map/stb,tab->sta/dot_general | solution.py:53
  673.0 2.0 fusion.22
  675.0 1.0 copy.44
  676.0 34.1 %reduce-scatter.5.cloned.1.call-done = f32[64,256]{1,0:T(8,128)} async-done(((f32[64,2048]{1,0:T(8,128)}), f32[64,256]{1,0:T(8,128)}) %reduce-scatter.5.cloned.1.call-update) | async-done | bytes 65552 | tf_op jit(solution)/shard_map/reduce_scatter | solution.py:57
  710.1 1.1 convolution_subtract_fusion
  711.4 99.4 %psum.23 = f32[64,64]{0,1:T(8,128)S(1)} all-reduce(f32[64,64]{0,1:T(8,128)S(1)} %fusion.54), channel_id=1, replica_groups=mesh['row'=64,'col'=8] {'row','col'}, use_global_device_ids=true, to_apply=%region_6.8 | all-reduce | flops 4096 | bytes 32768 | tf_op jit(solution)/shard_map/psum | solution.py:60
  810.9 5.8 cholesky.55
  817.4 1.3 select_bitcast_fusion
  818.7 4.9 custom-call.9
  823.6 0.9 fusion.31
  (40 shorter events, 5.8 us)
Async XLA Ops:
  7.2 1.5 copy-start
  7.2 260.1 %reduce-scatter.3.cloned.1.call-start = ((), (), s32[]{:S(2)}) async-start(), calls=%async_computation.2 | async-start | bytes 2129920 | tf_op jit(solution)/shard_map/reduce_scatter | solution.py:45
  10.2 5.7 copy-start.5
  18.4 1.2 copy-start.3
  18.4 1.2 copy-start.4
  19.8 1.4 copy-start.1
  21.2 637.8 %all-gather.2.cloned.1.call-start = ((), (), s32[]{:S(2)}) async-start(), calls=%async_computation.3 | async-start | bytes 2129920 | tf_op jit(solution)/shard_map/all_gather | solution.py:49
  577.6 132.5 %copy-start.2 = (f32[64,64]{1,0:T(8,128)}, f32[64,64]{1,0:T(8,128)S(1)}, u32[]{:S(2)}) copy-start(f32[64,64]{1,0:T(8,128)S(1)} %get-tuple-element.8) | copy-start | bytes 49156
  584.2 125.9 %reduce-scatter.5.cloned.1.call-start = ((), (), s32[]{:S(2)}) async-start(), calls=%async_computation.4 | async-start | bytes 589824 | tf_op jit(solution)/shard_map/reduce_scatter | solution.py:57
  662.9 10.1 %copy-start.6 = (s32[1,1,64]{2,1,0:T(1,128)S(1)}, s32[1,1,64]{2,1,0:T(1,128)}, u32[]{:S(2)}) copy-start(s32[1,1,64]{2,1,0:T(1,128)} %param.9) | copy-start | bytes 772
Sparse Core Ops, SparseCore 0:
  21.3 245.9 reduce-scatter.2
  584.3 74.6 all-gather.1
  676.1 33.9 reduce-scatter.4
